TPU v7x, 512 devices: a whole 4x4x16 slice. The times are simulated.
512 devices in a mesh: tensor: 32 (over z_hi, x, core), seq: 16 (over z_lo, y).
Axes of the slice: x: 4, y: 4, z: 16 (z_hi: 4, z_lo: 4; z = z_hi * 4 + z_lo), core: 2. Of those that a mesh axis runs over, the one named last changes fastest.
Arguments:
- resid: bfloat16 [16, 512, 2048], P('seq', 'tensor'), may hold values from -6 to 6
- norm_gain: bfloat16 [2048], replicated, may hold values from 0.099609375 to 1.8984375
- gate_weight_matrix: bfloat16 [2048, 10944], P(None, 'tensor'), may hold values from -0.125 to 0.125
- up_weight: bfloat16 [2048, 10944], P(None, 'tensor'), may hold values from -0.125 to 0.125
- w_down: bfloat16 [10944, 2048], P('tensor'), may hold values from -0.0546875 to 0.0546875
- gate_a: bfloat16 [64, 2048, 16], P('seq', 'tensor'), may hold values from -0.125 to 0.125
- gate_b: bfloat16 [64, 16, 10944], P('seq', None, 'tensor'), may hold values from -1.5 to 1.5
- up_a: bfloat16 [64, 2048, 16], P('seq', 'tensor'), may hold values from -0.125 to 0.125
- up_b: bfloat16 [64, 16, 10944], P('seq', None, 'tensor'), may hold values from -1.5 to 1.5
- down_a: bfloat16 [64, 10944, 16], P('seq', 'tensor'), may hold values from -0.0546875 to 0.0546875
- down_b: bfloat16 [64, 16, 2048], P('seq'), may hold values from -1.5 to 1.5
- prompt_lengths: int32 [16, 8], P('seq'), may hold values from 1 to 256, 512 in all within a row
- prompt_choice: int32 [16, 8], P('seq'), may hold values from 0 to 15
- used_adapters: int32 [16], replicated, may hold values from 0 to 63, as said below
- adapter_holder: int32 [64], replicated, may hold values from 0 to 63, each once
Outputs:
- output: bfloat16 [16, 512, 2048], P('seq', 'tensor')
Inputs may be any that keep to these rules, and one draw needn't show every extreme that they name: `used_adapters`: 16 distinct adapter ids.
All inputs are finite; a program needn't handle non-finite values.
Results may differ from a plain program's by a relative error of at most 0.017.
Values may be sent and summed in bfloat16 or wider, within the bound.
No kernel may reach another device: no remote copies, remote signals or barrier semaphores. Data moves between devices by JAX's collectives and lax.ppermute only.
A program may use at most 128 MiB of HBM per device.

v0:
```python
import jax
import jax.numpy as jnp
from jax import lax
from jax.sharding import PartitionSpec as P

adapter_scale = 0.5


def choose(picker, stacked):
    flat = stacked.reshape(stacked.shape[0], -1)
    chosen = jnp.dot(picker, flat, preferred_element_type=jnp.float32).astype(jnp.bfloat16)
    return chosen.reshape((picker.shape[0],) + stacked.shape[1:])


def to_columns(stacked):
    used_n, inner, rank_n = stacked.shape
    return jnp.transpose(stacked, (1, 0, 2)).reshape(inner, used_n * rank_n)


def local(
    resid,
    norm_gain,
    gate_weight_matrix,
    up_weight,
    w_down,
    gate_a,
    gate_b,
    up_a,
    up_b,
    down_a,
    down_b,
    prompt_lengths,
    prompt_choice,
    used_adapters,
    adapter_holder,
):
    tensor_n = lax.axis_size("tensor")
    tok_dev = resid.shape[1]
    group_tok = tok_dev * tensor_n
    used_n = used_adapters.shape[0]
    rank_n = gate_a.shape[2]
    feat_loc = gate_a.shape[1]
    hidden_local = gate_weight_matrix.shape[1]
    adapters_n = adapter_holder.shape[0]
    matches = used_adapters[:, None] == jnp.arange(adapters_n, dtype=jnp.int32)[None, :]
    slot_used = jnp.sum(jnp.where(matches, adapter_holder[None, :], 0), axis=1)
    whole = (
        lax.all_gather(gate_a, "seq", axis=0, tiled=True),
        lax.all_gather(up_a, "seq", axis=0, tiled=True),
        lax.all_gather(gate_b, "seq", axis=0, tiled=True),
        lax.all_gather(up_b, "seq", axis=0, tiled=True),
        lax.all_gather(down_a, "seq", axis=0, tiled=True),
        lax.all_gather(down_b, "seq", axis=0, tiled=True),
    )
    picker = (slot_used[:, None] == jnp.arange(adapters_n, dtype=jnp.int32)[None, :]).astype(
        jnp.bfloat16
    )
    fetched = tuple((choose(picker, stacked) for stacked in whole))
    fetch_ga, fetch_ua, fetch_gb, fetch_ub, fetch_da, fetch_db = fetched
    prompt_ends = jnp.cumsum(prompt_lengths[0])
    positions = jnp.arange(group_tok, dtype=jnp.int32)
    prompt_index = jnp.sum((positions[:, None] >= prompt_ends[None, :]).astype(jnp.int32), axis=1)
    prompts_n = prompt_lengths.shape[1]
    hits = prompt_index[:, None] == jnp.arange(prompts_n, dtype=jnp.int32)[None, :]
    tok_choice = jnp.sum(jnp.where(hits, prompt_choice[0][None, :], 0), axis=1)
    token_weights = (tok_choice[:, None] == jnp.arange(used_n, dtype=jnp.int32)[None, :]).astype(
        jnp.float32
    )
    row_first = lax.axis_index("tensor") * tok_dev
    own_weights = lax.dynamic_slice_in_dim(token_weights, row_first, tok_dev, 0)
    residual_float = resid[0].astype(jnp.float32)
    scale = lax.rsqrt(jnp.mean(residual_float * residual_float, axis=-1, keepdims=True) + 1e-06)
    normalized_input = (residual_float * scale * norm_gain.astype(jnp.float32)).astype(jnp.bfloat16)
    both_in = jnp.concatenate([to_columns(fetch_ga), to_columns(fetch_ua)], axis=1)
    col_first = lax.axis_index("tensor") * feat_loc
    piece = lax.all_gather(normalized_input, "tensor", axis=0, tiled=True)
    gate_part = jnp.dot(piece, gate_weight_matrix, preferred_element_type=jnp.float32)
    up_part = jnp.dot(piece, up_weight, preferred_element_type=jnp.float32)
    own_cols = lax.dynamic_slice_in_dim(piece, col_first, feat_loc, 1)
    low_part = jnp.dot(own_cols, both_in, preferred_element_type=jnp.float32)
    joined = jnp.concatenate([gate_part, up_part, low_part], axis=1)
    plain_output = joined[:, : 2 * hidden_local]
    low_rank = joined[:, 2 * hidden_local :].reshape(group_tok, 2, used_n, rank_n)
    partial_mid = jnp.sum(low_rank * token_weights[:, None, :, None], axis=2)
    mids = lax.psum(partial_mid.astype(jnp.bfloat16), "tensor")
    weights_bf = token_weights.astype(jnp.bfloat16)
    spread = (mids[:, :, None, :] * weights_bf[:, None, :, None]).reshape(
        group_tok, 2, used_n * rank_n
    )
    gate_adapter_rows = jnp.dot(
        spread[:, 0],
        fetch_gb.reshape(used_n * rank_n, hidden_local),
        preferred_element_type=jnp.float32,
    )
    up_adapter_rows = jnp.dot(
        spread[:, 1],
        fetch_ub.reshape(used_n * rank_n, hidden_local),
        preferred_element_type=jnp.float32,
    )
    gate_preactivation = plain_output[:, :hidden_local] + adapter_scale * gate_adapter_rows
    up_preactivation = plain_output[:, hidden_local:] + adapter_scale * up_adapter_rows
    hidden = (jax.nn.silu(gate_preactivation) * up_preactivation).astype(jnp.bfloat16)
    down_total_sum = lax.psum_scatter(
        jnp.dot(hidden, w_down, preferred_element_type=jnp.float32).astype(jnp.bfloat16),
        "tensor",
        scatter_dimension=0,
        tiled=True,
    ).astype(jnp.float32)
    down_adapter_rows = jnp.dot(
        hidden, to_columns(fetch_da), preferred_element_type=jnp.float32
    ).reshape(group_tok, used_n, rank_n)
    partial_down = jnp.sum(down_adapter_rows * token_weights[:, :, None], axis=1)
    mid_down = lax.psum_scatter(
        partial_down.astype(jnp.bfloat16), "tensor", scatter_dimension=0, tiled=True
    )
    spread_down = (mid_down[:, None, :] * own_weights.astype(jnp.bfloat16)[:, :, None]).reshape(
        tok_dev, used_n * rank_n
    )
    adapter_down_term = jnp.dot(
        spread_down,
        fetch_db.reshape(used_n * rank_n, fetch_db.shape[2]),
        preferred_element_type=jnp.float32,
    )
    return (residual_float + down_total_sum + adapter_scale * adapter_down_term).astype(
        jnp.bfloat16
    )[None]


def solution(mesh):
    placed = (
        P("seq", "tensor", None),
        P(),
        P(None, "tensor"),
        P(None, "tensor"),
        P("tensor", None),
        P("seq", "tensor", None),
        P("seq", None, "tensor"),
        P("seq", "tensor", None),
        P("seq", None, "tensor"),
        P("seq", "tensor", None),
        P("seq", None, None),
        P("seq", None),
        P("seq", None),
        P(),
        P(),
    )
    return jax.shard_map(
        local, mesh=mesh, in_specs=placed, out_specs=P("seq", "tensor", None), check_vma=False
    )
```

profile of v0, /device:TPU:8, one launch (start us, length us, event | category | flops | bytes accessed | tf_op | source)
XLA Modules:
  0.0 651.8 jit_solution(14810793064661548938)
XLA Ops:
  7.4 1.1 fusion.10
  8.5 0.7 convert_element_type.78
  9.2 1.5 fusion.12
  10.8 1.3 reduce-window.8
  12.1 44.3 %all_gather.22 = bf16[64,64,16]{1,2,0:T(8,128)(2,1)S(1)} all-gather(bf16[4,64,16]{1,2,0:T(8,128)(2,1)} %param.20), channel_id=1, replica_groups=mesh['tensor'=32,'seq'=16] {'seq'}, dimensions={0}, use_global_device_ids=true | all-gather | bytes 139264 | tf_op jit(solution)/shard_map/all_gather | solution.py:48
  56.4 0.4 copy.47
  56.8 0.9 select_reduce_fusion.1
  57.7 0.2 convolution_convert_fusion.6
  57.9 0.2 reshape.158
  58.1 0.1 copy.48
  58.3 44.6 %all_gather.23 = bf16[64,64,16]{1,2,0:T(8,128)(2,1)S(1)} all-gather(bf16[4,64,16]{1,2,0:T(8,128)(2,1)} %param.22), channel_id=1, replica_groups=mesh['tensor'=32,'seq'=16] {'seq'}, dimensions={0}, use_global_device_ids=true | all-gather | bytes 139264 | tf_op jit(solution)/shard_map/all_gather | solution.py:49
  102.9 0.4 copy.49
  103.3 0.2 convolution_convert_fusion.5
  103.5 0.2 reshape.161
  103.7 0.1 copy.50
  103.9 40.5 %all_gather.24 = bf16[64,16,342]{2,1,0:T(8,128)(2,1)S(1)} all-gather(bf16[4,16,342]{2,1,0:T(8,128)(2,1)S(1)} %copy-done.2), channel_id=1, replica_groups=mesh['tensor'=32,'seq'=16] {'seq'}, dimensions={0}, use_global_device_ids=true | all-gather | bytes 744192 | tf_op jit(solution)/shard_map/all_gather | solution.py:50
  144.4 0.7 reshape.166
  145.1 0.3 convolution_convert_fusion.3
  145.4 0.3 reshape_reshape.9
  145.7 44.4 %all_gather.25 = bf16[64,16,342]{2,1,0:T(8,128)(2,1)S(1)} all-gather(bf16[4,16,342]{2,1,0:T(8,128)(2,1)S(1)} %copy-done.3), channel_id=1, replica_groups=mesh['tensor'=32,'seq'=16] {'seq'}, dimensions={0}, use_global_device_ids=true | all-gather | bytes 744192 | tf_op jit(solution)/shard_map/all_gather | solution.py:51
  190.1 0.7 reshape.167
  190.9 0.3 convolution_convert_fusion.2
  191.1 1.0 reshape_reshape.10
  192.1 43.4 %all_gather.26 = bf16[64,342,16]{1,2,0:T(8,128)(2,1)} all-gather(bf16[4,342,16]{1,2,0:T(8,128)(2,1)S(1)} %copy-done.4), channel_id=1, replica_groups=mesh['tensor'=32,'seq'=16] {'seq'}, dimensions={0}, use_global_device_ids=true | all-gather | bytes 744192 | tf_op jit(solution)/shard_map/all_gather | solution.py:52
  235.6 2.4 copy.53
  238.0 0.5 convolution_convert_fusion.1
  238.5 1.1 reshape.169
  239.6 0.6 copy.54
  240.5 1.4 fusion.13
  241.9 0.1 multiply_reduce_fusion
  242.0 167.8 %psum.7 = bf16[512,2,16]{0,2,1:T(8,128)(2,1)S(1)} all-reduce(bf16[512,2,16]{0,2,1:T(8,128)(2,1)S(1)} %multiply_reduce_fusion), channel_id=1, replica_groups=mesh['tensor'=32,'seq'=16] {'tensor'}, use_global_device_ids=true, to_apply=%region_6.7 | all-reduce | flops 16384 | bytes 65536 | tf_op jit(solution)/shard_map/psum | solution.py:85
  409.9 2.7 fusion.28
  412.6 0.3 fusion.5
  412.9 0.9 fusion.29
  413.9 0.4 fusion.6
  414.2 0.3 fusion.7
  414.6 0.8 copy.57
  415.4 0.5 all-gather.5.cloned.1.call-update
  415.9 0.2 reduce-scatter.5.cloned.1.call-start
  416.1 2.6 convolution_convert_fusion.4
  419.0 103.0 %reduce-scatter.7.cloned.1.call-done = bf16[16,16]{1,0:T(8,128)(2,1)} async-done(((bf16[512,16]{1,0:T(8,128)(2,1)}), bf16[16,16]{1,0:T(8,128)(2,1)}) %reduce-scatter.7.cloned.1.call-update) | async-done | bytes 528 | tf_op jit(solution)/shard_map/reduce_scatter | solution.py:113
  522.0 0.8 broadcast_multiply_fusion
  522.8 0.1 mul.127
  522.9 4.6 copy.59
  527.5 0.7 convolution_convert_fusion
  528.2 0.5 reshape_reshape.11
  528.8 114.1 %reduce-scatter.5.cloned.1.call-done = bf16[16,2048]{1,0:T(8,128)(2,1)} async-done(((bf16[512,2048]{1,0:T(8,128)(2,1)}), bf16[16,2048]{1,0:T(8,128)(2,1)}) %reduce-scatter.5.cloned.1.call-update) | async-done | bytes 65552 | tf_op jit(solution)/shard_map/reduce_scatter | solution.py:103
  642.9 1.8 fusion.2
  (36 shorter events, 0.6 us)
Async XLA Ops:
  7.4 408.8 %copy-start = (bf16[342,2048]{1,0:T(8,128)(2,1)S(1)}, bf16[342,2048]{1,0:T(8,128)(2,1)}, u32[]{:S(2)}) copy-start(bf16[342,2048]{1,0:T(8,128)(2,1)} %param.19) | copy-start | bytes 4202500
  7.4 96.5 %copy-start.2 = (bf16[4,16,342]{2,1,0:T(8,128)(2,1)S(1)}, bf16[4,16,342]{2,1,0:T(8,128)(2,1)}, u32[]{:S(2)}) copy-start(bf16[4,16,342]{2,1,0:T(8,128)(2,1)} %param.21) | copy-start | bytes 131332
  7.4 233.1 %all-gather.3.cloned.1.call-start = ((), (), s32[]{:S(2)}) async-start(), calls=%async_computation.2 | async-start | bytes 2162688 | tf_op jit(solution)/shard_map/all_gather | solution.py:76
  10.7 511.3 %reduce-scatter.7.cloned.1.call-start = ((), (), s32[]{:S(2)}) async-start(), calls=%async_computation.5 | async-start | bytes 135168 | tf_op jit(solution)/shard_map/reduce_scatter | solution.py:113
  103.5 42.3 %copy-start.3 = (bf16[4,16,342]{2,1,0:T(8,128)(2,1)S(1)}, bf16[4,16,342]{2,1,0:T(8,128)(2,1)}, u32[]{:S(2)}) copy-start(bf16[4,16,342]{2,1,0:T(8,128)(2,1)} %param.23) | copy-start | bytes 131332
  145.4 46.7 %copy-start.4 = (bf16[4,342,16]{1,2,0:T(8,128)(2,1)S(1)}, bf16[4,342,16]{1,2,0:T(8,128)(2,1)}, u32[]{:S(2)}) copy-start(bf16[4,342,16]{1,2,0:T(8,128)(2,1)} %param.24) | copy-start | bytes 131332
  238.0 2.2 copy-start.7
  238.0 2.3 copy-start.6
  240.2 169.6 %copy-start.8 = (bf16[2048,342]{0,1:T(8,128)(2,1)S(1)}, bf16[2048,342]{0,1:T(8,128)(2,1)}, u32[]{:S(2)}) copy-start(bf16[2048,342]{0,1:T(8,128)(2,1)} %param.17) | copy-start | bytes 4202500
  409.8 3.0 copy-start.5
  409.9 3.0 copy-start.9
  412.9 0.9 copy-start.1
  415.3 107.6 %all-gather.5.cloned.1.call-start = ((), (), s32[]{:S(2)}) async-start(), calls=%async_computation.4 | async-start | bytes 4456448 | tf_op jit(solution)/shard_map/all_gather | solution.py:53
  415.9 227.0 %reduce-scatter.5.cloned.1.call-start = ((), (), s32[]{:S(2)}) async-start(), calls=%async_computation.3 | async-start | bytes 2162688 | tf_op jit(solution)/shard_map/reduce_scatter | solution.py:103
Sparse Core Ops, SparseCore 0:
  11.3 83.0 all-gather.2
  415.4 106.5 reduce-scatter.6
  526.4 116.4 reduce-scatter.4
Sparse Core Ops, SparseCore 1:
  417.9 92.9 all-gather.4
where the time goes:
time: 652 us
  blocking collectives  385 us (59%)
  waiting for transfers between devices  218 us (33%)
  between operations  14.9 us (2%)
  local copies, waits for them, and re-layouts  14.7 us (2%)
  matrix products  12.5 us (2%)
  other arithmetic  6.66 us (1%)
    psum x1, blocking collectives, local(): mids = lax.psum(partial_mid.astype(jnp.bfloat16), 'tensor')  168 us
    reduce_scatter x1, waiting for transfers between devices, local(): lax.psum_scatter(jnp.dot(hidden, w_down, preferred_element_type=jnp.float...  114 us
    reduce_scatter x1, waiting for transfers between devices, local(): lax.psum_scatter(partial_down.astype(jnp.bfloat16), 'tensor', scatter_dim...  103 us
    all_gather x1, blocking collectives, local(): lax.all_gather(up_a, 'seq', axis=0, tiled=True)  44.6 us
    all_gather x1, blocking collectives, local(): lax.all_gather(up_b, 'seq', axis=0, tiled=True)  44.4 us
    all_gather x1, blocking collectives, local(): lax.all_gather(gate_a, 'seq', axis=0, tiled=True)  44.3 us
    all_gather x1, blocking collectives, local(): lax.all_gather(down_a, 'seq', axis=0, tiled=True)  43.4 us
    all_gather x1, blocking collectives, local(): lax.all_gather(gate_b, 'seq', axis=0, tiled=True)  40.5 us
  transfers between devices with their start and end apart: 4, of which 2 were waited for; matrix products, arithmetic and copies ran while one was open for 3% of the time, Pallas kernels for 0%

commit v1 on v0

--- a/solution.py
+++ b/solution.py
@@ -82,7 +82,7 @@
     plain_output = joined[:, : 2 * hidden_local]
     low_rank = joined[:, 2 * hidden_local :].reshape(group_tok, 2, used_n, rank_n)
     partial_mid = jnp.sum(low_rank * token_weights[:, None, :, None], axis=2)
-    mids = lax.psum(partial_mid.astype(jnp.bfloat16), "tensor")
+    mids = jnp.sum(lax.all_gather(partial_mid.astype(jnp.bfloat16), "tensor"), axis=0)
     weights_bf = token_weights.astype(jnp.bfloat16)
     spread = (mids[:, :, None, :] * weights_bf[:, None, :, None]).reshape(
         group_tok, 2, used_n * rank_n

time: 652 us -> 498 us (0.76)
  blocking collectives: 385 us -> 220 us
    psum x1 -> x0, blocking collectives: 168 us -> none  [local(): mids = lax.psum(partial_mid.astype(jnp.bfloat16), 'tensor')]
  transfers between devices with their start and end apart: 4 -> 5, of which waited for: 2 -> 2; matrix products, arithmetic and copies ran while one was open for 3% -> 5% of each run, Pallas kernels for 0% -> 0%
where the time goes in v1:
time: 498 us; the launch traced here: 497 us
  waiting for transfers between devices  221 us (44%)
  blocking collectives  220 us (44%)
  local copies, waits for them, and re-layouts  17.4 us (3%)
  between operations  14.9 us (3%)
  matrix products  13.6 us (3%)
  other arithmetic  9 us (2%)
    reduce_scatter x1, waiting for transfers between devices, local(): lax.psum_scatter(jnp.dot(hidden, w_down, preferred_element_type=jnp.float...  114 us
    reduce_scatter x1, waiting for transfers between devices, local(): lax.psum_scatter(partial_down.astype(jnp.bfloat16), 'tensor', scatter_dim...  107 us
    all_gather x1, blocking collectives, local(): lax.all_gather(down_a, 'seq', axis=0, tiled=True)  46.3 us
    all_gather x1, blocking collectives, local(): lax.all_gather(gate_a, 'seq', axis=0, tiled=True)  44.6 us
    all_gather x1, blocking collectives, local(): lax.all_gather(up_a, 'seq', axis=0, tiled=True)  44.5 us
    all_gather x1, blocking collectives, local(): lax.all_gather(up_b, 'seq', axis=0, tiled=True)  44.2 us
    all_gather x1, blocking collectives, local(): lax.all_gather(gate_b, 'seq', axis=0, tiled=True)  40.7 us
  transfers between devices with their start and end apart: 5, of which 2 were waited for; matrix products, arithmetic and copies ran while one was open for 5% of the time, Pallas kernels for 0%

profile of v1, /device:TPU:8, one launch (start us, length us, event | category | flops | bytes accessed | tf_op | source)
XLA Modules:
  0.0 497.0 jit_solution(15082653465271481542)
XLA Ops:
  7.4 1.1 fusion.10
  8.5 0.7 convert_element_type.90
  9.2 1.5 fusion.12
  10.8 0.8 reduce-window.8
  11.6 44.6 %all_gather.26 = bf16[64,64,16]{1,2,0:T(8,128)(2,1)S(1)} all-gather(bf16[4,64,16]{1,2,0:T(8,128)(2,1)} %param.20), channel_id=1, replica_groups=mesh['tensor'=32,'seq'=16] {'seq'}, dimensions={0}, use_global_device_ids=true | all-gather | bytes 139264 | tf_op jit(solution)/shard_map/all_gather | solution.py:48
  56.2 0.4 copy.47
  56.6 0.9 select_reduce_fusion.1
  57.7 0.2 reshape.166
  58.1 44.5 %all_gather.27 = bf16[64,64,16]{1,2,0:T(8,128)(2,1)S(1)} all-gather(bf16[4,64,16]{1,2,0:T(8,128)(2,1)} %param.22), channel_id=1, replica_groups=mesh['tensor'=32,'seq'=16] {'seq'}, dimensions={0}, use_global_device_ids=true | all-gather | bytes 139264 | tf_op jit(solution)/shard_map/all_gather | solution.py:49
  102.5 0.4 copy.49
  103.1 0.2 reshape.169
  103.5 40.7 %all_gather.29 = bf16[64,16,342]{2,1,0:T(8,128)(2,1)S(1)} all-gather(bf16[4,16,342]{2,1,0:T(8,128)(2,1)S(1)} %copy-done.4), channel_id=1, replica_groups=mesh['tensor'=32,'seq'=16] {'seq'}, dimensions={0}, use_global_device_ids=true | all-gather | bytes 744192 | tf_op jit(solution)/shard_map/all_gather | solution.py:50
  144.2 0.7 reshape.174
  145.1 0.6 fusion.19
  145.8 1.3 fusion.13
  147.0 0.7 multiply_reduce_fusion
  147.9 0.3 convolution_convert_fusion.3
  148.1 0.3 reshape_reshape.9
  148.5 44.2 %all_gather.30 = bf16[64,16,342]{2,1,0:T(8,128)(2,1)S(1)} all-gather(bf16[4,16,342]{2,1,0:T(8,128)(2,1)S(1)} %copy-done.5), channel_id=1, replica_groups=mesh['tensor'=32,'seq'=16] {'seq'}, dimensions={0}, use_global_device_ids=true | all-gather | bytes 744192 | tf_op jit(solution)/shard_map/all_gather | solution.py:51
  192.7 0.7 reshape.175
  193.5 0.3 convolution_convert_fusion.2
  193.7 1.0 reshape_reshape.10
  194.7 46.3 %all_gather.31 = bf16[64,342,16]{1,2,0:T(8,128)(2,1)} all-gather(bf16[4,342,16]{1,2,0:T(8,128)(2,1)S(1)} %copy-done.6), channel_id=1, replica_groups=mesh['tensor'=32,'seq'=16] {'seq'}, dimensions={0}, use_global_device_ids=true | all-gather | bytes 744192 | tf_op jit(solution)/shard_map/all_gather | solution.py:52
  241.0 2.4 copy.53
  243.5 0.5 convolution_convert_fusion.1
  244.0 1.1 reshape.177
  245.0 0.6 copy.54
  245.7 3.9 fusion.29
  249.6 0.9 fusion.28
  250.6 1.5 copy.59
  252.1 0.9 reduce_sum.71
  253.0 0.8 mul.113
  253.8 0.8 bitcast_multiply_fusion
  254.6 0.3 fusion.5
  255.0 0.4 fusion.6
  255.4 0.4 copy-done.3
  255.7 0.3 fusion.7
  256.0 0.8 copy.57
  256.9 0.5 all-gather.7.cloned.1.call-update
  257.4 0.2 reduce-scatter.5.cloned.1.call-start
  257.6 2.6 convolution_convert_fusion.4
  260.4 106.8 %reduce-scatter.7.cloned.1.call-done = bf16[16,16]{1,0:T(8,128)(2,1)} async-done(((bf16[512,16]{1,0:T(8,128)(2,1)}), bf16[16,16]{1,0:T(8,128)(2,1)}) %reduce-scatter.7.cloned.1.call-update) | async-done | bytes 528 | tf_op jit(solution)/shard_map/reduce_scatter | solution.py:113
  367.3 0.8 broadcast_multiply_fusion
  368.2 4.6 copy.60
  372.8 0.7 convolution_convert_fusion
  373.5 0.5 reshape_reshape.11
  374.1 114.0 %reduce-scatter.5.cloned.1.call-done = bf16[16,2048]{1,0:T(8,128)(2,1)} async-done(((bf16[512,2048]{1,0:T(8,128)(2,1)}), bf16[16,2048]{1,0:T(8,128)(2,1)}) %reduce-scatter.5.cloned.1.call-update) | async-done | bytes 65552 | tf_op jit(solution)/shard_map/reduce_scatter | solution.py:103
  488.1 1.8 fusion.2
  (46 shorter events, 1.4 us)
Async XLA Ops:
  7.4 250.3 %copy-start = (bf16[342,2048]{1,0:T(8,128)(2,1)S(1)}, bf16[342,2048]{1,0:T(8,128)(2,1)}, u32[]{:S(2)}) copy-start(bf16[342,2048]{1,0:T(8,128)(2,1)} %param.19) | copy-start | bytes 4202500
  7.4 96.1 %copy-start.4 = (bf16[4,16,342]{2,1,0:T(8,128)(2,1)S(1)}, bf16[4,16,342]{2,1,0:T(8,128)(2,1)}, u32[]{:S(2)}) copy-start(bf16[4,16,342]{2,1,0:T(8,128)(2,1)} %param.21) | copy-start | bytes 131332
  7.4 138.4 %all-gather.5.cloned.1.call-start = ((), (), s32[]{:S(2)}) async-start(), calls=%async_computation.2 | async-start | bytes 2162688 | tf_op jit(solution)/shard_map/all_gather | solution.py:76
  10.7 239.8 %all-gather.9.cloned.1.call-start = ((), (), s32[]{:S(2)}) async-start(), calls=%async_computation.5 | async-start | bytes 1081344 | tf_op jit(solution)/shard_map/all_gather | solution.py:85
  57.5 186.0 %copy-start.7 = (s32[16]{0:T(128)}, s32[16]{0:T(128)S(1)}, u32[]{:S(2)}) copy-start(s32[16]{0:T(128)S(1)} %select_reduce_fusion.1) | copy-start | bytes 196
  58.0 87.0 %copy-start.10 = (s32[1,8]{1,0:T(1,128)S(1)}, s32[1,8]{1,0:T(1,128)}, u32[]{:S(2)}) copy-start(s32[1,8]{1,0:T(1,128)} %param.27) | copy-start | bytes 100
  145.0 3.5 copy-start.5
  145.8 2.0 copy-start.2
  147.8 219.4 %reduce-scatter.7.cloned.1.call-start = ((), (), s32[]{:S(2)}) async-start(), calls=%async_computation.6 | async-start | bytes 135168 | tf_op jit(solution)/shard_map/reduce_scatter | solution.py:113
  148.1 46.6 %copy-start.6 = (bf16[4,342,16]{1,2,0:T(8,128)(2,1)S(1)}, bf16[4,342,16]{1,2,0:T(8,128)(2,1)}, u32[]{:S(2)}) copy-start(bf16[4,342,16]{1,2,0:T(8,128)(2,1)} %param.24) | copy-start | bytes 131332
  245.7 3.9 copy-start.9
  245.7 3.9 copy-start.11
  253.0 1.9 copy-start.1
  253.0 1.9 copy-start.12
  255.0 0.8 copy-start.3
  256.8 111.4 %all-gather.7.cloned.1.call-start = ((), (), s32[]{:S(2)}) async-start(), calls=%async_computation.4 | async-start | bytes 4456448 | tf_op jit(solution)/shard_map/all_gather | solution.py:53
  257.4 230.7 %reduce-scatter.5.cloned.1.call-start = ((), (), s32[]{:S(2)}) async-start(), calls=%async_computation.3 | async-start | bytes 2162688 | tf_op jit(solution)/shard_map/reduce_scatter | solution.py:103
  368.2 4.6 copy-start.8
Sparse Core Ops, SparseCore 0:
  11.3 82.9 all-gather.4
  147.9 77.4 all-gather.8
  256.9 110.2 reduce-scatter.6
  371.5 116.4 reduce-scatter.4
Sparse Core Ops, SparseCore 1:
  259.4 96.6 all-gather.6
